TPU v7x, 256 devices: a whole 4x4x8 slice. The times are simulated.
256 devices in a mesh: row: 16 (over z, core), col: 16 (over y, x).
Axes of the slice: x: 4, y: 4, z: 8, core: 2. Of those that a mesh axis runs over, the one named last changes fastest.
Arguments:
- matrix: bfloat16 [4096, 262144], P('row', 'col'), may hold values from -60 to 60
- test_matrix: bfloat16 [262144, 512], P(('col', 'row')), may hold values from -0.0390625 to 0.0390625
Outputs:
- orthonormal: float32 [4096, 512], P(('row', 'col'))
- triangular: float32 [512, 512], replicated
All inputs are finite; a program needn't handle non-finite values.
Results may differ from a plain program's by a relative error of at most 0.0003.
Values may be sent and summed in bfloat16 or wider, within the bound.
No kernel may reach another device: no remote copies, remote signals or barrier semaphores. Data moves between devices by JAX's collectives and lax.ppermute only.
A program may use at most 128 MiB of HBM per device.

v0:
```python
import jax
import jax.numpy as jnp
from jax import lax
from jax.sharding import PartitionSpec as P


def probe_product(matrix, test_matrix):
    return jnp.dot(
        matrix,
        lax.all_gather(test_matrix, "row", axis=0, tiled=True),
        preferred_element_type=jnp.float32,
    )


def gram_term(own_rows):
    return jnp.dot(own_rows.T, own_rows, precision=lax.Precision.HIGHEST)


def shards(matrix, test_matrix):
    share_rows = matrix.shape[0] // lax.axis_size("col")
    total_rows = matrix.shape[0] * lax.axis_size("row")
    partial_value = probe_product(matrix, test_matrix)
    sketch = lax.psum(partial_value, "col")
    gram = lax.psum(gram_term(sketch), "row")
    own_rows = lax.dynamic_slice_in_dim(sketch, lax.axis_index("col") * share_rows, share_rows, 0)
    gram = gram / jnp.float32(total_rows)
    lower_factor = jnp.linalg.cholesky(gram)
    orthonormal = lax.linalg.triangular_solve(
        lower_factor, own_rows, left_side=False, lower=True, transpose_a=True
    )
    return (orthonormal, lower_factor.T)


def solution(mesh):
    in_specs = (P("row", "col"), P(("col", "row"), None))
    out_specs = (P(("row", "col"), None), P())
    return jax.shard_map(shards, mesh=mesh, in_specs=in_specs, out_specs=out_specs, check_vma=False)
```

profile of v0, /device:TPU:1, one launch (start us, length us, event | category | flops | bytes accessed | tf_op | source)
XLA Modules:
  0.0 478.8 jit_solution(10044351522613762331)
XLA Ops:
  7.2 0.0 all-gather.2.cloned.1.call-start
  7.2 0.7 all-gather.2.cloned.1.call-update
  7.9 0.0 all-reduce.4.cloned.1.call-start
  7.9 101.4 %all-gather.2.cloned.1.call-done = bf16[16384,512]{1,0:T(8,128)(2,1)} async-done(((bf16[1024,512]{1,0:T(8,128)(2,1)}), bf16[16384,512]{1,0:T(8,128)(2,1)}) %all-gather.2.cloned.1.call-update) | async-done | bytes 16777232 | tf_op jit(solution)/shard_map/all_gather | solution.py:10
  109.4 13.4 %fusion.34 = f32[256,512]{1,0:T(8,128)} fusion(bf16[256,16384]{1,0:T(8,128)(2,1)} %param.2, bf16[16384,512]{1,0:T(8,128)(2,1)} %all-gather.2.cloned.1.call-done), kind=kOutput, calls=%fused_computation.71 | convolution fusion | flops 4294967296 | bytes 25690112 | tf_op jit(solution)/shard_map/dot_general | solution.py:8
  122.8 0.0 all-reduce.4.cloned.1.call-update
  122.8 0.2 all-reduce.6.cloned.1.call-start
  123.1 91.7 %all-reduce.4.cloned.1.call-done = f32[256,512]{1,0:T(8,128)} async-done(((f32[256,512]{1,0:T(8,128)}), f32[256,512]{1,0:T(8,128)}) %all-reduce.4.cloned.1.call-update) | async-done | bytes 524304 | tf_op jit(solution)/shard_map/psum | solution.py:23
  214.8 3.2 fusion.35
  218.0 0.0 all-reduce.6.cloned.1.call-update
  218.1 113.7 %all-reduce.6.cloned.1.call-done = f32[512,512]{0,1:T(8,128)} async-done(((f32[512,512]{0,1:T(8,128)}), f32[512,512]{0,1:T(8,128)}) %all-reduce.6.cloned.1.call-update) | async-done | bytes 1048592 | tf_op jit(solution)/shard_map/psum | solution.py:24
  331.8 1.3 broadcast_multiply_fusion
  333.1 0.3 copy.5
  333.5 1.5 fusion
  334.9 11.7 %cholesky.104 = f32[128,128]{1,0:T(8,128)S(1)} custom-call(f32[128,128]{1,0:T(8,128)S(1)} %cholesky.266), custom_call_target="Cholesky" | custom-call | tf_op jit(solution)/shard_map/jit(cholesky)/cholesky | solution.py:27
  346.7 9.8 %custom-call.30 = f32[1,128,128]{1,2,0:T(8,128)S(1)} custom-call(f32[1,128,128]{2,1,0:T(8,128)S(1)} %get-tuple-element.33), custom_call_target="InvertDiagBlocksLowerTriangular" | custom-call | tf_op jit(solution)/shard_map/jit(cholesky)/cholesky | solution.py:27
  356.5 0.1 cholesky.224
  356.6 0.3 constant_dynamic-update-slice_fusion.2
  357.0 0.3 convolution_subtract_fusion
  357.3 11.8 %cholesky.217 = f32[128,128]{1,0:T(8,128)S(1)} custom-call(f32[128,128]{1,0:T(8,128)S(1)} %cholesky.270), custom_call_target="Cholesky" | custom-call | tf_op jit(solution)/shard_map/jit(cholesky)/cholesky | solution.py:27
  369.2 9.8 %custom-call.31 = f32[1,128,128]{1,2,0:T(8,128)S(1)} custom-call(f32[1,128,128]{2,1,0:T(8,128)S(1)} %get-tuple-element.30), custom_call_target="InvertDiagBlocksLowerTriangular" | custom-call | tf_op jit(solution)/shard_map/jit(cholesky)/cholesky | solution.py:27
  379.0 0.3 convolution_dynamic-update-slice_fusion
  379.3 0.4 convolution_subtract_fusion.1
  379.7 11.7 %cholesky.238 = f32[128,128]{1,0:T(8,128)S(1)} custom-call(f32[128,128]{1,0:T(8,128)S(1)} %cholesky.275), custom_call_target="Cholesky" | custom-call | tf_op jit(solution)/shard_map/jit(cholesky)/cholesky | solution.py:27
  391.4 0.7 compare_reduce_fusion.1
  392.1 9.8 %custom-call.32 = f32[1,128,128]{1,2,0:T(8,128)S(1)} custom-call(f32[1,128,128]{2,1,0:T(8,128)S(1)} %get-tuple-element.27), custom_call_target="InvertDiagBlocksLowerTriangular" | custom-call | tf_op jit(solution)/shard_map/jit(cholesky)/cholesky | solution.py:27
  402.0 0.2 convolution_dynamic-update-slice_fusion.1
  402.2 0.4 convolution_subtract_fusion.2
  402.6 12.0 %cholesky.255 = f32[128,128]{1,0:T(8,128)S(1)} custom-call(f32[128,128]{1,0:T(8,128)S(1)} %convolution_subtract_fusion.2), custom_call_target="Cholesky" | custom-call | tf_op jit(solution)/shard_map/jit(cholesky)/cholesky | solution.py:27
  414.6 0.6 compare_reduce_fusion
  415.2 0.7 compare_reduce_fusion.2
  418.4 0.3 fusion.2
  418.7 1.3 copy.6
  420.0 8.1 %while.1 = (s32[]{:T(128)}, f32[512,512]{1,0:T(8,128)S(1)}, s32[4,2]{0,1:T(2,128)S(1)}, f32[4,128,128]{2,1,0:T(8,128)S(1)}, s32[]{:T(128)}) while((s32[]{:T(128)}, f32[512,512]{1,0:T(8,128)S(1)}, s32[4,2]{0,1:T(2,128)S(1)}, f32[4,128,128]{2,1,0:T(8,128)S(1)}, s32[]{:T(128)}) %tuple.33), condition=%wide.while_cond, body=%wide.while_body.sunk | while | flops 2 | bytes 131181 | solution.py:28
  420.0 0.1 constant_dynamic-slice_fusion.2
  420.0 0.6 fusion.46
  420.6 1.3 bitcast_dynamic-update-slice_fusion.2
  422.0 0.1 constant_dynamic-slice_fusion.2
  422.1 0.6 fusion.46
  422.7 1.3 bitcast_dynamic-update-slice_fusion.2
  424.0 0.1 constant_dynamic-slice_fusion.2
  424.1 0.6 fusion.46
  424.7 1.3 bitcast_dynamic-update-slice_fusion.2
  426.1 0.1 constant_dynamic-slice_fusion.2
  426.2 0.6 fusion.46
  426.8 1.3 bitcast_dynamic-update-slice_fusion.2
  428.1 39.3 %custom-call.33 = f32[4,128,128]{1,2,0:T(8,128)S(1)} custom-call(f32[4,128,128]{2,1,0:T(8,128)S(1)} %get-tuple-element.9), custom_call_target="InvertDiagBlocksLowerTriangular" | custom-call | tf_op jit(solution)/shard_map/triangular_solve | solution.py:28
  467.4 0.9 fusion.15
  468.3 0.9 convolution_subtract_fusion.5
  469.2 0.2 fusion.13
  469.4 0.9 convolution_subtract_fusion.4
  470.3 0.2 fusion.12
  470.5 1.0 convolution_subtract_fusion.3
  471.5 0.2 fusion.11
  471.7 0.6 pad_maximum_fusion
  (10 shorter events, 0.2 us)
Async XLA Ops:
  7.2 102.2 %all-gather.2.cloned.1.call-start = ((), (), s32[]{:S(2)}) async-start(), calls=%async_computation | async-start | bytes 17825792 | tf_op jit(solution)/shard_map/all_gather | solution.py:10
  7.9 206.9 %all-reduce.4.cloned.1.call-start = ((), (), s32[]{:S(2)}) async-start(), calls=%async_computation.1 | async-start | bytes 1048576 | tf_op jit(solution)/shard_map/psum | solution.py:23
  122.8 209.0 %all-reduce.6.cloned.1.call-start = ((), (), s32[]{:S(2)}) async-start(), calls=%async_computation.2 | async-start | bytes 2097152 | tf_op jit(solution)/shard_map/psum | solution.py:24
Sparse Core Ops, SparseCore 0:
  9.8 99.5 all-gather.1
  123.0 91.8 all-reduce.3
  218.2 113.5 all-reduce.5
where the time goes:
time: 479 us
  waiting for transfers between devices  308 us (64%)
  other arithmetic  122 us (25%)
  matrix products  22.7 us (5%)
  between operations  16.5 us (3%)
  local copies, waits for them, and re-layouts  9.84 us (2%)
    psum x1, waiting for transfers between devices, shards(): gram = lax.psum(gram_term(sketch), 'row')  114 us
    all_gather x1, waiting for transfers between devices, probe_product(): lax.all_gather(test_matrix, 'row', axis=0, tiled=True)  101 us
    psum x1, waiting for transfers between devices, shards(): sketch = lax.psum(partial_value, 'col')  91.7 us
    another operation x14, other arithmetic, shards(): lower_factor = jnp.linalg.cholesky(gram)  78.8 us
    another operation x3, other arithmetic, shards(): lax.linalg.triangular_solve(lower_factor, own_rows, left_side=False, lowe...  40 us
    dot_general x1, matrix products, probe_product(): jnp.dot(matrix, lax.all_gather(test_matrix, 'row', axis=0, tiled=True), p...  13.4 us
  transfers between devices with their start and end apart: 3, of which 3 were waited for; matrix products, arithmetic and copies ran while one was open for 0% of the time, Pallas kernels for 0%

commit v1 on v0

--- a/solution.py
+++ b/solution.py
@@ -20,7 +20,9 @@
     share_rows = matrix.shape[0] // lax.axis_size("col")
     total_rows = matrix.shape[0] * lax.axis_size("row")
     partial_value = probe_product(matrix, test_matrix)
-    sketch = lax.psum(partial_value, "col")
+    sketch = partial_value
+    for hop in (1, 2, 4, 8):
+        sketch = sketch + lax.ppermute(sketch, "col", [(dev, dev ^ hop) for dev in range(16)])
     gram = lax.psum(gram_term(sketch), "row")
     own_rows = lax.dynamic_slice_in_dim(sketch, lax.axis_index("col") * share_rows, share_rows, 0)
     gram = gram / jnp.float32(total_rows)

time: 479 us -> 440 us (0.919)
  waiting for transfers between devices: 308 us -> 259 us
  starting transfers between devices: 0.3 us -> 8.43 us
    psum x1 -> x0, waiting for transfers between devices: 91.7 us -> none  [shards(): sketch = lax.psum(partial_value, 'col')]
    ppermute x0 -> x4, waiting for transfers between devices: none -> 43 us  [shards(): lax.ppermute(sketch, 'col', [(dev, dev ^ hop) for dev in range(16)])]
    ppermute x0 -> x4, starting transfers between devices: none -> 8.35 us  [shards(): lax.ppermute(sketch, 'col', [(dev, dev ^ hop) for dev in range(16)])]
  transfers between devices with their start and end apart: 3 -> 6, of which waited for: 3 -> 6; matrix products, arithmetic and copies ran while one was open for 0% -> 0% of each run, Pallas kernels for 0% -> 0%
where the time goes in v1:
time: 440 us; the launch traced here: 439 us
  waiting for transfers between devices  259 us (59%)
  other arithmetic  123 us (28%)
  matrix products  18.5 us (4%)
  between operations  16.8 us (4%)
  local copies, waits for them, and re-layouts  13.4 us (3%)
  starting transfers between devices  8.43 us (2%)
    psum x1, waiting for transfers between devices, shards(): gram = lax.psum(gram_term(sketch), 'row')  114 us
    all_gather x1, waiting for transfers between devices, probe_product(): lax.all_gather(test_matrix, 'row', axis=0, tiled=True)  101 us
    another operation x14, other arithmetic, shards(): lower_factor = jnp.linalg.cholesky(gram)  78.8 us
    ppermute x4, waiting for transfers between devices, shards(): lax.ppermute(sketch, 'col', [(dev, dev ^ hop) for dev in range(16)])  43 us
    another operation x3, other arithmetic, shards(): lax.linalg.triangular_solve(lower_factor, own_rows, left_side=False, lowe...  40 us
    another operation x12, local copies, waits for them, and re-layouts  11.6 us
    dot_general x1, matrix products, probe_product(): jnp.dot(matrix, lax.all_gather(test_matrix, 'row', axis=0, tiled=True), p...  10.5 us
  transfers between devices with their start and end apart: 6, of which 6 were waited for; matrix products, arithmetic and copies ran while one was open for 0% of the time, Pallas kernels for 0%

profile of v1, /device:TPU:1, one launch (start us, length us, event | category | flops | bytes accessed | tf_op | source)
XLA Modules:
  0.0 439.1 jit_solution(10984597754903419416)
XLA Ops:
  7.2 0.0 all-gather.2.cloned.1.call-start
  7.2 0.7 all-gather.2.cloned.1.call-update
  7.9 0.0 all-reduce.3.cloned.1.call-start
  7.9 101.4 %all-gather.2.cloned.1.call-done = bf16[16384,512]{1,0:T(8,128)(2,1)} async-done(((bf16[1024,512]{1,0:T(8,128)(2,1)}), bf16[16384,512]{1,0:T(8,128)(2,1)}) %all-gather.2.cloned.1.call-update) | async-done | bytes 16777232 | tf_op jit(solution)/shard_map/all_gather | solution.py:10
  109.4 10.5 %fusion.37 = f32[256,512]{1,0:T(8,128)S(1)} fusion(bf16[256,16384]{1,0:T(8,128)(2,1)} %param.2, bf16[16384,512]{1,0:T(8,128)(2,1)} %all-gather.2.cloned.1.call-done), kind=kOutput, calls=%fused_computation.74 | convolution fusion | flops 4294967296 | bytes 25690112 | tf_op jit(solution)/shard_map/dot_general | solution.py:8
  119.9 1.3 collective-permute-start
  121.2 12.0 %collective-permute-done = f32[256,512]{1,0:T(8,128)S(1)} collective-permute-done((f32[256,512]{1,0:T(8,128)S(1)}, f32[256,512]{1,0:T(8,128)S(1)}, u32[]{:S(2)}, u32[]{:S(2)}) %collective-permute-start) | collective-permute-done | bytes 524320 | tf_op jit(solution)/shard_map/ppermute | solution.py:25
  133.2 0.1 add.57
  133.3 2.8 collective-permute-start.1
  136.1 11.2 %collective-permute-done.1 = f32[256,512]{1,0:T(8,128)S(1)} collective-permute-done((f32[256,512]{1,0:T(8,128)S(1)}, f32[256,512]{1,0:T(8,128)S(1)}, u32[]{:S(2)}, u32[]{:S(2)}) %collective-permute-start.1) | collective-permute-done | bytes 524320 | tf_op jit(solution)/shard_map/ppermute | solution.py:25
  147.2 0.1 add.58
  147.3 1.3 collective-permute-start.2
  148.6 10.3 %collective-permute-done.2 = f32[256,512]{1,0:T(8,128)S(1)} collective-permute-done((f32[256,512]{1,0:T(8,128)S(1)}, f32[256,512]{1,0:T(8,128)S(1)}, u32[]{:S(2)}, u32[]{:S(2)}) %collective-permute-start.2) | collective-permute-done | bytes 524320 | tf_op jit(solution)/shard_map/ppermute | solution.py:25
  158.9 0.1 add.59
  159.0 3.0 collective-permute-start.3
  162.0 9.5 %collective-permute-done.3 = f32[256,512]{1,0:T(8,128)S(1)} collective-permute-done((f32[256,512]{1,0:T(8,128)S(1)}, f32[256,512]{1,0:T(8,128)S(1)}, u32[]{:S(2)}, u32[]{:S(2)}) %collective-permute-start.3) | collective-permute-done | bytes 524320 | tf_op jit(solution)/shard_map/ppermute | solution.py:25
  171.5 0.1 add.60
  171.6 2.0 fusion.38
  173.6 0.0 all-reduce.3.cloned.1.call-update
  173.7 113.7 %all-reduce.3.cloned.1.call-done = f32[512,512]{0,1:T(8,128)} async-done(((f32[512,512]{0,1:T(8,128)}), f32[512,512]{0,1:T(8,128)}) %all-reduce.3.cloned.1.call-update) | async-done | bytes 1048592 | tf_op jit(solution)/shard_map/psum | solution.py:26
  287.4 1.3 broadcast_multiply_fusion
  288.7 0.3 copy.5
  289.0 1.5 fusion
  290.5 11.7 %cholesky.104 = f32[128,128]{1,0:T(8,128)S(1)} custom-call(f32[128,128]{1,0:T(8,128)S(1)} %cholesky.266), custom_call_target="Cholesky" | custom-call | tf_op jit(solution)/shard_map/jit(cholesky)/cholesky | solution.py:29
  302.3 9.8 %custom-call.30 = f32[1,128,128]{1,2,0:T(8,128)S(1)} custom-call(f32[1,128,128]{2,1,0:T(8,128)S(1)} %get-tuple-element.33), custom_call_target="InvertDiagBlocksLowerTriangular" | custom-call | tf_op jit(solution)/shard_map/jit(cholesky)/cholesky | solution.py:29
  312.1 0.1 cholesky.224
  312.2 0.3 constant_dynamic-update-slice_fusion.2
  312.5 0.3 convolution_subtract_fusion
  312.9 11.9 %cholesky.217 = f32[128,128]{1,0:T(8,128)S(1)} custom-call(f32[128,128]{1,0:T(8,128)S(1)} %cholesky.270), custom_call_target="Cholesky" | custom-call | tf_op jit(solution)/shard_map/jit(cholesky)/cholesky | solution.py:29
  324.8 9.8 %custom-call.31 = f32[1,128,128]{1,2,0:T(8,128)S(1)} custom-call(f32[1,128,128]{2,1,0:T(8,128)S(1)} %get-tuple-element.30), custom_call_target="InvertDiagBlocksLowerTriangular" | custom-call | tf_op jit(solution)/shard_map/jit(cholesky)/cholesky | solution.py:29
  334.6 0.3 convolution_dynamic-update-slice_fusion
  334.9 0.4 convolution_subtract_fusion.1
  335.2 11.7 %cholesky.238 = f32[128,128]{1,0:T(8,128)S(1)} custom-call(f32[128,128]{1,0:T(8,128)S(1)} %cholesky.275), custom_call_target="Cholesky" | custom-call | tf_op jit(solution)/shard_map/jit(cholesky)/cholesky | solution.py:29
  347.0 0.7 compare_reduce_fusion.1
  347.7 9.8 %custom-call.32 = f32[1,128,128]{1,2,0:T(8,128)S(1)} custom-call(f32[1,128,128]{2,1,0:T(8,128)S(1)} %get-tuple-element.27), custom_call_target="InvertDiagBlocksLowerTriangular" | custom-call | tf_op jit(solution)/shard_map/jit(cholesky)/cholesky | solution.py:29
  357.5 0.2 convolution_dynamic-update-slice_fusion.1
  357.7 0.4 convolution_subtract_fusion.2
  358.1 11.9 %cholesky.255 = f32[128,128]{1,0:T(8,128)S(1)} custom-call(f32[128,128]{1,0:T(8,128)S(1)} %convolution_subtract_fusion.2), custom_call_target="Cholesky" | custom-call | tf_op jit(solution)/shard_map/jit(cholesky)/cholesky | solution.py:29
  370.1 0.6 compare_reduce_fusion
  370.7 0.7 compare_reduce_fusion.2
  373.9 1.3 fusion.2
  375.2 1.3 copy.6
  376.5 11.7 %while.1 = (s32[]{:T(128)}, f32[512,512]{1,0:T(8,128)}, s32[4,2]{0,1:T(2,128)S(1)}, f32[4,128,128]{2,1,0:T(8,128)S(1)}, s32[]{:T(128)}) while((s32[]{:T(128)}, f32[512,512]{1,0:T(8,128)}, s32[4,2]{0,1:T(2,128)S(1)}, f32[4,128,128]{2,1,0:T(8,128)S(1)}, s32[]{:T(128)}) %tuple.33), condition=%wide.while_cond, body=%wide.while_body.sunk | while | flops 2 | bytes 131181 | solution.py:30
  376.5 0.1 constant_dynamic-slice_fusion.2
  376.6 0.6 fusion.46
  377.2 2.3 bitcast_dynamic-update-slice_fusion.2
  379.4 0.1 constant_dynamic-slice_fusion.2
  379.5 0.6 fusion.46
  380.1 2.3 bitcast_dynamic-update-slice_fusion.2
  382.4 0.1 constant_dynamic-slice_fusion.2
  382.5 0.6 fusion.46
  383.1 2.3 bitcast_dynamic-update-slice_fusion.2
  385.3 0.1 constant_dynamic-slice_fusion.2
  385.4 0.6 fusion.46
  386.0 2.2 bitcast_dynamic-update-slice_fusion.2
  388.2 39.3 %custom-call.33 = f32[4,128,128]{1,2,0:T(8,128)S(1)} custom-call(f32[4,128,128]{2,1,0:T(8,128)S(1)} %get-tuple-element.9), custom_call_target="InvertDiagBlocksLowerTriangular" | custom-call | tf_op jit(solution)/shard_map/triangular_solve | solution.py:30
  427.5 0.2 fusion.18
  427.7 1.0 fusion.16
  428.7 0.2 fusion.15
  428.9 1.1 fusion.9
  430.0 0.2 fusion.14
  430.2 1.3 fusion.4
  431.5 0.2 fusion.13
  431.6 0.6 pad_maximum_fusion
  (10 shorter events, 0.2 us)
Async XLA Ops:
  7.2 102.2 %all-gather.2.cloned.1.call-start = ((), (), s32[]{:S(2)}) async-start(), calls=%async_computation | async-start | bytes 17825792 | tf_op jit(solution)/shard_map/all_gather | solution.py:10
  7.9 279.5 %all-reduce.3.cloned.1.call-start = ((), (), s32[]{:S(2)}) async-start(), calls=%async_computation.1 | async-start | bytes 2097152 | tf_op jit(solution)/shard_map/psum | solution.py:26
  119.9 13.3 %collective-permute-start = (f32[256,512]{1,0:T(8,128)S(1)}, f32[256,512]{1,0:T(8,128)S(1)}, u32[]{:S(2)}, u32[]{:S(2)}) collective-permute-start(f32[256,512]{1,0:T(8,128)S(1)} %fusion.37), channel_id=1, source_target_pairs={{0,1},{1,0},{2,3},{3,2},{4,5},{5,4},{6,7},{7,6},{8,9},{9,8},{10,11... | collective-permute-start | bytes 1572872 | tf_op jit(solution)/shard_map/ppermute | solution.py:25
  133.3 14.0 %collective-permute-start.1 = (f32[256,512]{1,0:T(8,128)S(1)}, f32[256,512]{1,0:T(8,128)S(1)}, u32[]{:S(2)}, u32[]{:S(2)}) collective-permute-start(f32[256,512]{1,0:T(8,128)S(1)} %add.57), channel_id=1, source_target_pairs={{0,2},{1,3},{2,0},{3,1},{4,6},{5,7},{6,4},{7,5},{8,10},{9,11},{10,... | collective-permute-start | bytes 1572872 | tf_op jit(solution)/shard_map/ppermute | solution.py:25
  147.3 11.6 %collective-permute-start.2 = (f32[256,512]{1,0:T(8,128)S(1)}, f32[256,512]{1,0:T(8,128)S(1)}, u32[]{:S(2)}, u32[]{:S(2)}) collective-permute-start(f32[256,512]{1,0:T(8,128)S(1)} %add.58), channel_id=1, source_target_pairs={{0,4},{1,5},{2,6},{3,7},{4,0},{5,1},{6,2},{7,3},{8,12},{9,13},{10,... | collective-permute-start | bytes 1572872 | tf_op jit(solution)/shard_map/ppermute | solution.py:25
  159.0 12.5 %collective-permute-start.3 = (f32[256,512]{1,0:T(8,128)S(1)}, f32[256,512]{1,0:T(8,128)S(1)}, u32[]{:S(2)}, u32[]{:S(2)}) collective-permute-start(f32[256,512]{1,0:T(8,128)S(1)} %add.59), channel_id=1, source_target_pairs={{0,8},{1,9},{2,10},{3,11},{4,12},{5,13},{6,14},{7,15},{8,0},{9,1},... | collective-permute-start | bytes 1572872 | tf_op jit(solution)/shard_map/ppermute | solution.py:25
Sparse Core Ops, SparseCore 0:
  9.8 99.5 all-gather.1
  173.8 113.5 all-reduce.2
